TPU v7x, 256 devices: a whole 4x4x8 slice. The times are simulated.
256 devices in a mesh: ctx: 16 (over y_lo, z), exp: 8 (over x, core), rep: 2 (over y_hi).
Axes of the slice: x: 4, y: 4 (y_hi: 2, y_lo: 2; y = y_hi * 2 + y_lo), z: 8, core: 2. Of those that a mesh axis runs over, the one named last changes fastest.
Arguments:
- sequence: bfloat16 [2, 2048, 2048], P('rep', 'ctx'), may hold values from -6 to 6
- norm1_gain: float32 [2048], replicated, may hold values from 0.1 to 1.9
- w_in: bfloat16 [2048, 3, 2048], P(None, None, 'exp'), may hold values from -0.125 to 0.125
- long_filter: float32 [2048, 2048], P('ctx', 'exp'), may hold values from -0.125 to 0.125
- filter_decay: float32 [2048], P('exp'), may hold values from 0.5 to 150
- conv_bias: float32 [2048], P('exp'), may hold values from -4 to 4
- w_out: bfloat16 [2048, 2048], P('exp'), may hold values from -0.125 to 0.125
- norm2_gain: float32 [2048], replicated, may hold values from 0.1 to 1.9
- router: bfloat16 [2048, 8], replicated, may hold values from -0.39648438 to 0.39648438
- w_gate: bfloat16 [8, 2048, 4096], P('exp', None, 'ctx'), may hold values from -0.125 to 0.125
- w_up: bfloat16 [8, 2048, 4096], P('exp', None, 'ctx'), may hold values from -0.125 to 0.125
- w_down: bfloat16 [8, 4096, 2048], P('exp', 'ctx'), may hold values from -0.09375 to 0.09375
- experts: int32 [2, 2048, 2], P('rep', ('ctx', 'exp')), may hold values from 0 to 7, as said below
- expert_slots: int32 [2, 2048, 2], P('rep', ('ctx', 'exp')), may hold values from 0 to 7, as said below
- splice_head: bfloat16 [112, 2048], replicated, may hold values from -0.125 to 0.125
- targets: float32 [2, 2048, 112], P('rep', ('ctx', 'exp')), may hold values from 0 to 1
Outputs:
- block_out: bfloat16 [2, 2048, 2048], P('rep', ('ctx', 'exp'))
- head_grad: float32 [112, 2048], replicated
Inputs may be any that keep to these rules, and one draw needn't show every extreme that they name: Each token names two different experts. Among the tokens of one aligned block of 16 tokens, no expert is named more than 8 times, and in each replica one expert is named exactly 8 times in every block. `expert_slots`: A choice's slot is the number of choices of the same expert before it within its aligned block of 16 tokens, in token order, a token's first choice before its second.
All inputs are finite; a program needn't handle non-finite values.
Results may differ from a plain program's by a relative error of at most 0.011.
Values may be sent and summed in bfloat16 or wider, within the bound.
No kernel may reach another device: no remote copies, remote signals or barrier semaphores. Data moves between devices by JAX's collectives and lax.ppermute only.
A program may use at most 64 MiB of HBM per device.

v0:
```python
import math

import jax
import jax.numpy as jnp
from jax import lax
from jax.sharding import PartitionSpec as P

TWO_PI = 2.0 * math.pi


def stored(values):
    return lax.optimization_barrier(values.astype(jnp.bfloat16))


def rms_scale(token_rows, norm_gain):
    wide = token_rows.astype(jnp.float32)
    inverse = lax.rsqrt(jnp.mean(wide * wide, axis=-1, keepdims=True) + 1e-05)
    return (wide * inverse * norm_gain).astype(jnp.bfloat16)


def phase_table(first_ids, second_ids, modulus):
    angle = (
        TWO_PI * (first_ids[:, None] * second_ids[None, :] % modulus).astype(jnp.float32) / modulus
    )
    return (jnp.cos(angle), jnp.sin(angle))


def spectra_move(blocks):
    return lax.all_to_all(blocks, "ctx", split_axis=0, concat_axis=1, tiled=True)


def token_move(blocks):
    return lax.all_to_all(blocks, ("ctx", "exp"), split_axis=0, concat_axis=0, tiled=True)


def causal_convolve(source, shaped):
    highest = lax.Precision.HIGHEST
    ctx_count = lax.axis_size("ctx")
    ctx_pos = lax.axis_index("ctx")
    local_rows, channels = source.shape
    sub_rows = local_rows // ctx_count
    halves = 2 * ctx_count
    points = halves * local_rows
    block_ids = jnp.arange(ctx_count, dtype=jnp.int32)
    freq_ids = jnp.arange(halves, dtype=jnp.int32)
    cos_outer, sin_outer = phase_table(block_ids, freq_ids, halves)
    gathered = spectra_move(jnp.stack([source, shaped], axis=1)).reshape(
        sub_rows, ctx_count, 2, channels
    )
    real_a = jnp.einsum("qcmx,ck->kqmx", gathered, cos_outer, precision=highest)
    imag_a = -jnp.einsum("qcmx,ck->kqmx", gathered, sin_outer, precision=highest)
    positions = ctx_pos * sub_rows + jnp.arange(sub_rows, dtype=jnp.int32)
    cos_twist, sin_twist = phase_table(freq_ids, positions, points)
    cos_twist = cos_twist[:, :, None, None]
    sin_twist = sin_twist[:, :, None, None]
    real_b = real_a * cos_twist + imag_a * sin_twist
    imag_b = imag_a * cos_twist - real_a * sin_twist
    spread = spectra_move(jnp.concatenate([real_b, imag_b], axis=2))
    row_ids = jnp.arange(local_rows, dtype=jnp.int32)
    cos_inner, sin_inner = phase_table(row_ids, row_ids, local_rows)
    cos_part = jnp.einsum("kpzx,pq->kqzx", spread, cos_inner, precision=highest)
    sin_part = jnp.einsum("kpzx,pq->kqzx", spread, sin_inner, precision=highest)
    real_f = cos_part[:, :, 0:2] + sin_part[:, :, 2:4]
    imag_f = cos_part[:, :, 2:4] - sin_part[:, :, 0:2]
    real_z = real_f[:, :, 0] * real_f[:, :, 1] - imag_f[:, :, 0] * imag_f[:, :, 1]
    imag_z = real_f[:, :, 0] * imag_f[:, :, 1] + imag_f[:, :, 0] * real_f[:, :, 1]
    product = jnp.stack([real_z, imag_z], axis=2)
    cos_back = jnp.einsum("kqrx,qp->pkrx", product, cos_inner, precision=highest)
    sin_back = jnp.einsum("kqrx,qp->pkrx", product, sin_inner, precision=highest)
    real_w = cos_back[:, :, 0] - sin_back[:, :, 1]
    imag_w = cos_back[:, :, 1] + sin_back[:, :, 0]
    returned = spectra_move(jnp.stack([real_w, imag_w], axis=2))
    cos_again, sin_again = phase_table(positions, freq_ids, points)
    cos_again = cos_again[:, :, None]
    sin_again = sin_again[:, :, None]
    real_v = returned[:, :, 0] * cos_again - returned[:, :, 1] * sin_again
    imag_v = returned[:, :, 1] * cos_again + returned[:, :, 0] * sin_again
    blocks_out = (
        jnp.einsum("qkx,ck->cqx", real_v, cos_outer, precision=highest)
        - jnp.einsum("qkx,ck->cqx", imag_v, sin_outer, precision=highest)
    ) / points
    return spectra_move(blocks_out)[0]


def shards(
    sequence,
    norm1_gain,
    w_in,
    long_filter,
    filter_decay,
    conv_bias,
    w_out,
    norm2_gain,
    router,
    w_gate,
    w_up,
    w_down,
    experts,
    expert_slots,
    splice_head,
    targets,
):
    exp_count = lax.axis_size("exp")
    exp_pos = lax.axis_index("exp")
    ctx_count = lax.axis_size("ctx")
    ctx_pos = lax.axis_index("ctx")
    local_x = sequence[0]
    local_rows, model_width = local_x.shape
    own_rows = local_rows // exp_count
    length = local_rows * ctx_count
    normed = rms_scale(local_x, norm1_gain)
    projected = jnp.einsum("ti,igd->tgd", normed, w_in, preferred_element_type=jnp.float32)
    source = projected[:, 1] * projected[:, 0]
    positions = (ctx_pos * local_rows + jnp.arange(local_rows, dtype=jnp.int32)).astype(jnp.float32)
    shaped = long_filter * jnp.exp(-filter_decay[None, :] * positions[:, None] / length)
    convolved = causal_convolve(source, shaped)
    gated_rows = (projected[:, 2] * (convolved + conv_bias[None, :] * source)).astype(jnp.bfloat16)
    mixed_sum = lax.psum_scatter(
        jnp.dot(gated_rows, w_out, preferred_element_type=jnp.float32),
        "exp",
        scatter_dimension=0,
        tiled=True,
    )
    residual_rows = lax.dynamic_slice_in_dim(local_x, exp_pos * own_rows, own_rows, 0)
    hidden_state = stored(residual_rows.astype(jnp.float32) + mixed_sum)
    routed_in = rms_scale(hidden_state, norm2_gain)
    chances = jax.nn.sigmoid(jnp.dot(routed_in, router, preferred_element_type=jnp.float32))
    picked_ids = experts[0]
    slot_ids = expert_slots[0]
    chosen = jnp.take_along_axis(chances, picked_ids, axis=1)
    weights = chosen / jnp.sum(chosen, axis=1, keepdims=True)
    n_experts = router.shape[1]
    capacity = 4 * own_rows // exp_count
    slot_rows = picked_ids * capacity + slot_ids
    buffer_ids = jnp.arange(n_experts * capacity, dtype=jnp.int32)[:, None]
    selector = (
        (slot_rows[None, :, 0] == buffer_ids) | (slot_rows[None, :, 1] == buffer_ids)
    ).astype(jnp.bfloat16)
    outgoing = jnp.dot(selector, routed_in, preferred_element_type=jnp.float32).astype(jnp.bfloat16)
    outgoing = outgoing.reshape(n_experts, capacity, model_width)
    gate_local = w_gate[0]
    up_local = w_up[0]
    down_local = w_down[0]
    copies = jnp.broadcast_to(outgoing[None], (ctx_count, n_experts, capacity, model_width))
    arrived = token_move(copies.reshape(ctx_count * n_experts, capacity, model_width))
    token_rows = arrived.reshape(-1, model_width)
    gate_val = jnp.dot(token_rows, gate_local, preferred_element_type=jnp.float32)
    up_val = jnp.dot(token_rows, up_local, preferred_element_type=jnp.float32)
    slice_hidden = (jax.nn.silu(gate_val) * up_val).astype(jnp.bfloat16)
    slice_part = (
        jnp.dot(slice_hidden, down_local, preferred_element_type=jnp.float32)
        .astype(jnp.bfloat16)
        .reshape(ctx_count * n_experts, capacity, model_width)
    )
    came_back = token_move(slice_part)
    summed = jnp.sum(
        came_back.reshape(ctx_count, n_experts, capacity, model_width).astype(jnp.float32), axis=0
    )
    expert_out = stored(summed)
    flat_out = expert_out.reshape(n_experts * capacity, model_width)
    first_rows = jnp.take(flat_out, slot_rows[:, 0], axis=0).astype(jnp.float32)
    second_rows = jnp.take(flat_out, slot_rows[:, 1], axis=0).astype(jnp.float32)
    combined = weights[:, 0:1] * first_rows + weights[:, 1:2] * second_rows
    block_final = stored(hidden_state.astype(jnp.float32) + combined)
    usage_prob = jax.nn.sigmoid(
        jnp.einsum("td,od->to", block_final, splice_head, preferred_element_type=jnp.float32)
    )
    all_tokens = lax.axis_size("rep") * ctx_count * exp_count * own_rows
    loss_scale = 1.0 / math.sqrt(all_tokens)
    usage_grad = ((usage_prob - targets[0]) * loss_scale).astype(jnp.bfloat16)
    local_grad = jnp.einsum(
        "to,td->od", usage_grad, block_final, preferred_element_type=jnp.float32
    )
    head_total = lax.psum(local_grad, ("ctx", "exp", "rep"))
    return (block_final[None], head_total)


def solution(mesh):
    in_specs = (
        P("rep", "ctx", None),
        P(),
        P(None, None, "exp"),
        P("ctx", "exp"),
        P("exp"),
        P("exp"),
        P("exp", None),
        P(),
        P(),
        P("exp", None, "ctx"),
        P("exp", None, "ctx"),
        P("exp", "ctx", None),
        P("rep", ("ctx", "exp"), None),
        P("rep", ("ctx", "exp"), None),
        P(),
        P("rep", ("ctx", "exp"), None),
    )
    out_specs = (P("rep", ("ctx", "exp"), None), P())
    return jax.shard_map(shards, mesh=mesh, in_specs=in_specs, out_specs=out_specs, check_vma=False)
```

profile of v0, /device:TPU:1, one launch (start us, length us, event | category | flops | bytes accessed | tf_op | source)
XLA Modules:
  0.0 642.9 jit_solution(7272265439014524673)
XLA Ops:
  7.2 1.4 fusion.22
  9.2 1.7 fusion.37
  12.8 10.1 %all-to-all-start = ((f32[128,2,256]{2,1,0:T(2,128)}), f32[128,2,256]{2,1,0:T(2,128)S(1)}, u32[]{:S(2)}, u32[]{:S(2)}) async-start(f32[128,2,256]{2,1,0:T(2,128)} %copy.38), calls=%async_computation | async-start | bytes 524288 | tf_op jit(solution)/shard_map/all_to_all | solution.py:29
  23.0 8.7 %all-to-all-done = f32[128,2,256]{2,1,0:T(2,128)S(1)} async-done(((f32[128,2,256]{2,1,0:T(2,128)}), f32[128,2,256]{2,1,0:T(2,128)S(1)}, u32[]{:S(2)}, u32[]{:S(2)}) %all-to-all-start) | async-done | bytes 262176 | tf_op jit(solution)/shard_map/all_to_all | solution.py:29
  34.0 29.2 %all_to_all.70 = f32[32,8,4,256]{3,2,1,0:T(4,128)S(1)} all-to-all(f32[32,8,4,256]{3,2,1,0:T(4,128)S(1)} %copy.41), channel_id=1, replica_groups=mesh['ctx'=16,'exp'=8,'rep'=2] {'ctx'}, dimensions={0} | all-to-all | bytes 2097152 | tf_op jit(solution)/shard_map/all_to_all | solution.py:29
  69.2 6.6 %all-to-all-start.2 = ((f32[128,2,2,256]{3,2,1,0:T(2,128)}), f32[128,2,2,256]{3,2,1,0:T(2,128)}, u32[]{:S(2)}, u32[]{:S(2)}) async-start(f32[128,2,2,256]{3,2,1,0:T(2,128)} %copy.43), calls=%async_computation.2 | async-start | bytes 1048576 | tf_op jit(solution)/shard_map/all_to_all | solution.py:29
  75.9 12.9 %all-to-all-done.2 = f32[128,2,2,256]{3,2,1,0:T(2,128)} async-done(((f32[128,2,2,256]{3,2,1,0:T(2,128)}), f32[128,2,2,256]{3,2,1,0:T(2,128)}, u32[]{:S(2)}, u32[]{:S(2)}) %all-to-all-start.2) | async-done | bytes 524320 | tf_op jit(solution)/shard_map/all_to_all | solution.py:29
  88.8 2.1 copy.44
  90.9 2.2 all_to_all.60
  93.1 1.4 fusion.51
  94.5 1.4 fusion.11
  96.0 13.4 %all_to_all.71 = f32[16,8,256]{2,1,0:T(8,128)S(1)} all-to-all(f32[16,8,256]{2,1,0:T(8,128)S(1)} %copy.45), channel_id=1, replica_groups=mesh['ctx'=16,'exp'=8,'rep'=2] {'ctx'}, dimensions={0} | all-to-all | bytes 262144 | tf_op jit(solution)/shard_map/all_to_all | solution.py:29
  109.4 2.6 fusion.72
  112.1 32.3 %reduce-scatter.2.cloned.1.call-done = f32[16,2048]{1,0:T(8,128)} async-done(((f32[128,2048]{1,0:T(8,128)}), f32[16,2048]{1,0:T(8,128)}) %reduce-scatter.2.cloned.1.call-update) | async-done | bytes 131088 | tf_op jit(solution)/shard_map/reduce_scatter | solution.py:118
  146.3 110.4 %all_to_all.72 = bf16[128,8,2048]{2,1,0:T(8,128)(2,1)S(1)} all-to-all(bf16[128,8,2048]{2,1,0:T(8,128)(2,1)S(1)} %bitcast.172), channel_id=1, replica_groups=mesh['ctx'=16,'exp'=8,'rep'=2] {'ctx','exp'}, dimensions={0} | all-to-all | bytes 8388608 | tf_op jit(solution)/shard_map/all_to_all | solution.py:33
  256.7 2.0 copy-done.1
  258.7 2.3 fusion.2
  261.0 9.4 %convert_bitcast_fusion = bf16[128,8,2048]{2,1,0:T(8,128)(2,1)} fusion(bf16[1,256,2048]{2,1,0:T(8,128)(2,1)} %param.29, bf16[128,8,2048]{2,1,0:T(8,128)(2,1)} %copy-done.1, bf16[1,2048,256]{2,1,0:T(8,128)(2,1)} %param.28, f32[1024,256]{1,0:T(8,128)} %fusion.2), kind=kOutput, calls=%fused_computation.7 | convolution fusion | flops 2151153664 | bytes 11534336 | tf_op jit(solution)/shard_map/dot_general | solution.py:151
  270.4 6.7 %all-to-all-start.5 = ((bf16[128,8,2048]{2,1,0:T(8,128)(2,1)}), bf16[128,8,2048]{2,1,0:T(8,128)(2,1)}, u32[]{:S(2)}, u32[]{:S(2)}) async-start(bf16[128,8,2048]{2,1,0:T(8,128)(2,1)} %convert_bitcast_fusion), calls=%async_computation.6 | async-start | bytes 8388608 | tf_op jit(solution)/shard_map/all_to_all | solution.py:33
  279.5 94.8 %all-to-all-done.5 = bf16[128,8,2048]{2,1,0:T(8,128)(2,1)} async-done(((bf16[128,8,2048]{2,1,0:T(8,128)(2,1)}), bf16[128,8,2048]{2,1,0:T(8,128)(2,1)}, u32[]{:S(2)}, u32[]{:S(2)}) %all-to-all-start.5) | async-done | bytes 4194336 | tf_op jit(solution)/shard_map/all_to_all | solution.py:33
  374.3 3.0 reduce_sum.42
  380.1 2.7 fusion.18
  382.9 251.0 %all-reduce.2.cloned.1.call-done = f32[112,2048]{1,0:T(8,128)} async-done(((f32[112,2048]{1,0:T(8,128)}), f32[112,2048]{1,0:T(8,128)}) %all-reduce.2.cloned.1.call-update) | async-done | bytes 917520 | tf_op jit(solution)/shard_map/psum | solution.py:174
  633.9 2.2 copy.73
  (75 shorter events, 18.1 us)
Async XLA Ops:
  7.2 2.1 copy-start
  7.2 4.5 copy-start.10
  7.2 4.5 copy-start.4
  10.9 0.8 copy-start.2
  12.8 18.9 %all-to-all-start = ((f32[128,2,256]{2,1,0:T(2,128)}), f32[128,2,256]{2,1,0:T(2,128)S(1)}, u32[]{:S(2)}, u32[]{:S(2)}) async-start(f32[128,2,256]{2,1,0:T(2,128)} %copy.38), calls=%async_computation | async-start | bytes 524288 | tf_op jit(solution)/shard_map/all_to_all | solution.py:29
  67.8 41.6 %copy-start.8 = (f32[256]{0:T(256)S(1)}, f32[256]{0:T(256)}, u32[]{:S(2)}) copy-start(f32[256]{0:T(256)} %param.23) | copy-start | bytes 3076
  69.1 42.9 %copy-start.5 = (s32[1,16,2]{1,2,0:T(2,128)S(1)}, s32[1,16,2]{1,2,0:T(2,128)}, u32[]{:S(2)}) copy-start(s32[1,16,2]{1,2,0:T(2,128)} %param.30) | copy-start | bytes 388
  69.1 42.9 %copy-start.9 = (s32[1,16,2]{1,2,0:T(2,128)S(1)}, s32[1,16,2]{1,2,0:T(2,128)}, u32[]{:S(2)}) copy-start(s32[1,16,2]{1,2,0:T(2,128)} %param.31) | copy-start | bytes 388
  69.1 76.3 %copy-start.7 = (f32[2048]{0:T(1024)S(1)}, f32[2048]{0:T(1024)}, u32[]{:S(2)}) copy-start(f32[2048]{0:T(1024)} %param.25) | copy-start | bytes 24580
  69.2 19.6 %all-to-all-start.2 = ((f32[128,2,2,256]{3,2,1,0:T(2,128)}), f32[128,2,2,256]{3,2,1,0:T(2,128)}, u32[]{:S(2)}, u32[]{:S(2)}) async-start(f32[128,2,2,256]{3,2,1,0:T(2,128)} %copy.43), calls=%async_computation.2 | async-start | bytes 1048576 | tf_op jit(solution)/shard_map/all_to_all | solution.py:29
  75.7 68.7 %reduce-scatter.2.cloned.1.call-start = ((), (), s32[]{:S(2)}) async-start(), calls=%async_computation.7 | async-start | bytes 1179648 | tf_op jit(solution)/shard_map/reduce_scatter | solution.py:118
  146.3 112.4 %copy-start.11 = (bf16[1,2048,256]{2,1,0:T(8,128)(2,1)S(1)}, bf16[1,2048,256]{2,1,0:T(8,128)(2,1)}, u32[]{:S(2)}) copy-start(bf16[1,2048,256]{2,1,0:T(8,128)(2,1)} %param.27) | copy-start | bytes 3145732
  256.7 2.0 copy-start.1
  270.4 7.4 %copy-start.12 = (bf16[2048,8]{0,1:T(8,128)(2,1)S(1)}, bf16[2048,8]{0,1:T(8,128)(2,1)}, u32[]{:S(2)}) copy-start(bf16[2048,8]{0,1:T(8,128)(2,1)} %param.26) | copy-start | bytes 98308
  270.4 103.9 %all-to-all-start.5 = ((bf16[128,8,2048]{2,1,0:T(8,128)(2,1)}), bf16[128,8,2048]{2,1,0:T(8,128)(2,1)}, u32[]{:S(2)}, u32[]{:S(2)}) async-start(bf16[128,8,2048]{2,1,0:T(8,128)(2,1)} %convert_bitcast_fusion), calls=%async_computation.6 | async-start | bytes 8388608 | tf_op jit(solution)/shard_map/all_to_all | solution.py:33
  277.1 356.8 %all-reduce.2.cloned.1.call-start = ((), (), s32[]{:S(2)}) async-start(), calls=%async_computation.8 | async-start | bytes 1835008 | tf_op jit(solution)/shard_map/psum | solution.py:174
  278.7 101.4 %copy-start.6 = (f32[1,16,112]{2,1,0:T(8,128)S(1)}, f32[1,16,112]{2,1,0:T(8,128)}, u32[]{:S(2)}) copy-start(f32[1,16,112]{2,1,0:T(8,128)} %param.33) | copy-start | bytes 21508
  380.1 256.0 %copy-start.3 = (bf16[16,2048]{1,0:T(8,128)(2,1)}, bf16[16,2048]{1,0:T(8,128)(2,1)S(1)}, u32[]{:S(2)}) copy-start(bf16[16,2048]{1,0:T(8,128)(2,1)S(1)} %fusion.60) | copy-start | bytes 196612
Sparse Core Ops, SparseCore 0:
  112.2 32.1 reduce-scatter.1
  383.0 250.8 all-reduce.1
where the time goes:
time: 644 us; the launch traced here: 643 us
  waiting for transfers between devices  400 us (62%)
  blocking collectives  153 us (24%)
  matrix products  27.8 us (4%)
  starting transfers between devices  23.4 us (4%)
  local copies, waits for them, and re-layouts  16.7 us (3%)
  between operations  14.4 us (2%)
  other arithmetic  7.75 us (1%)
    psum x1, waiting for transfers between devices, shards(): head_total = lax.psum(local_grad, ('ctx', 'exp', 'rep'))  251 us
    all_to_all x1, blocking collectives, token_move(): lax.all_to_all(blocks, ('ctx', 'exp'), split_axis=0, concat_axis=0, tiled...  110 us
    all_to_all x1, waiting for transfers between devices, token_move(): lax.all_to_all(blocks, ('ctx', 'exp'), split_axis=0, concat_axis=0, tiled...  94.8 us
    all_to_all x2, blocking collectives, spectra_move(): lax.all_to_all(blocks, 'ctx', split_axis=0, concat_axis=1, tiled=True)  42.7 us
    reduce_scatter x1, waiting for transfers between devices, shards(): lax.psum_scatter(jnp.dot(gated_rows, w_out, preferred_element_type=jnp.fl...  32.3 us
    all_to_all x2, waiting for transfers between devices, spectra_move(): lax.all_to_all(blocks, 'ctx', split_axis=0, concat_axis=1, tiled=True)  21.6 us
    all_to_all x2, starting transfers between devices, spectra_move(): lax.all_to_all(blocks, 'ctx', split_axis=0, concat_axis=1, tiled=True)  16.7 us
  transfers between devices with their start and end apart: 5, of which 5 were waited for; matrix products, arithmetic and copies ran while one was open for 0% of the time, Pallas kernels for 0%

commit v1 on v0

--- a/solution.py
+++ b/solution.py
@@ -27,6 +27,21 @@
 
 def spectra_move(blocks):
     return lax.all_to_all(blocks, "ctx", split_axis=0, concat_axis=1, tiled=True)
+
+
+def a2a_reduce(values, axes):
+    count = lax.axis_size(axes)
+    pieces = lax.all_to_all(values.reshape(count, -1), axes, 0, 0, tiled=True)
+    return jnp.sum(pieces, axis=0)
+
+
+def a2a_allreduce(values, axes):
+    count = lax.axis_size(axes)
+    if values.size % count:
+        return lax.psum(values, axes)
+    mine = a2a_reduce(values, axes)
+    spread = jnp.broadcast_to(mine[None], (count,) + mine.shape)
+    return lax.all_to_all(spread, axes, 0, 0, tiled=True).reshape(values.shape)
 
 
 def token_move(blocks):
@@ -115,11 +130,9 @@
     shaped = long_filter * jnp.exp(-filter_decay[None, :] * positions[:, None] / length)
     convolved = causal_convolve(source, shaped)
     gated_rows = (projected[:, 2] * (convolved + conv_bias[None, :] * source)).astype(jnp.bfloat16)
-    mixed_sum = lax.psum_scatter(
-        jnp.dot(gated_rows, w_out, preferred_element_type=jnp.float32),
-        "exp",
-        scatter_dimension=0,
-        tiled=True,
+    mixed_full = jnp.dot(gated_rows, w_out, preferred_element_type=jnp.float32)
+    mixed_sum = a2a_reduce(mixed_full.reshape(exp_count, own_rows * model_width), "exp").reshape(
+        own_rows, model_width
     )
     residual_rows = lax.dynamic_slice_in_dim(local_x, exp_pos * own_rows, own_rows, 0)
     hidden_state = stored(residual_rows.astype(jnp.float32) + mixed_sum)
@@ -171,7 +184,7 @@
     local_grad = jnp.einsum(
         "to,td->od", usage_grad, block_final, preferred_element_type=jnp.float32
     )
-    head_total = lax.psum(local_grad, ("ctx", "exp", "rep"))
+    head_total = a2a_allreduce(local_grad, ("ctx", "exp", "rep"))
     return (block_final[None], head_total)
 
 

time: 644 us -> 449 us (0.70)
  waiting for transfers between devices: 400 us -> 131 us
  blocking collectives: 153 us -> 217 us
  between operations: 14.4 us -> 1.03 us
  other arithmetic: 7.75 us -> 16.4 us
  starting transfers between devices: 23.4 us -> 31 us
  local copies, waits for them, and re-layouts: 16.7 us -> 24.2 us
    psum x1 -> x0, waiting for transfers between devices: 251 us -> none  [shards(): head_total = lax.psum(local_grad, ('ctx', 'exp', 'rep'))]
    all_to_all x0 -> x2, blocking collectives: none -> 70.1 us  [the longest x1 35.5 us: a2a_reduce(): pieces = lax.all_to_all(values.reshape(count, -1), axes, 0, 0, tiled=True)]
    reduce_scatter x1 -> x0, waiting for transfers between devices: 32.3 us -> none  [shards(): lax.psum_scatter(jnp.dot(gated_rows, w_out, preferred_element_type=jnp.fl...]
    all_to_all x0 -> x1, waiting for transfers between devices: none -> 15 us  [a2a_reduce(): pieces = lax.all_to_all(values.reshape(count, -1), axes, 0, 0, tiled=True)]
    all_to_all x0 -> x1, starting transfers between devices: none -> 7.61 us  [a2a_reduce(): pieces = lax.all_to_all(values.reshape(count, -1), axes, 0, 0, tiled=True)]
    all_to_all x0 -> x2, local copies, waits for them, and re-layouts: none -> 6.66 us  [a2a_reduce(): pieces = lax.all_to_all(values.reshape(count, -1), axes, 0, 0, tiled=True)]
    all_to_all x1, blocking collectives: 110 us -> 104 us  [token_move(): lax.all_to_all(blocks, ('ctx', 'exp'), split_axis=0, concat_axis=0, tiled...]
  transfers between devices with their start and end apart: 5 -> 4, of which waited for: 5 -> 4; matrix products, arithmetic and copies ran while one was open for 0% -> 1% of each run, Pallas kernels for 0% -> 0%
where the time goes in v1:
time: 449 us; the launch traced here: 448 us
  blocking collectives  217 us (48%)
  waiting for transfers between devices  131 us (29%)
  starting transfers between devices  31 us (7%)
  matrix products  27.8 us (6%)
  local copies, waits for them, and re-layouts  24.2 us (5%)
  other arithmetic  16.4 us (4%)
    all_to_all x1, blocking collectives, token_move(): lax.all_to_all(blocks, ('ctx', 'exp'), split_axis=0, concat_axis=0, tiled...  104 us
    all_to_all x1, waiting for transfers between devices, token_move(): lax.all_to_all(blocks, ('ctx', 'exp'), split_axis=0, concat_axis=0, tiled...  94 us
    all_to_all x2, blocking collectives, spectra_move(): lax.all_to_all(blocks, 'ctx', split_axis=0, concat_axis=1, tiled=True)  42.6 us
    all_to_all x1, blocking collectives, a2a_reduce(): pieces = lax.all_to_all(values.reshape(count, -1), axes, 0, 0, tiled=True)  35.5 us
    all_to_all x1, blocking collectives, a2a_allreduce(): return lax.all_to_all(spread, axes, 0, 0, tiled=True).reshape(values.shape)  34.6 us
    all_to_all x2, waiting for transfers between devices, spectra_move(): lax.all_to_all(blocks, 'ctx', split_axis=0, concat_axis=1, tiled=True)  21.6 us
    all_to_all x2, starting transfers between devices, spectra_move(): lax.all_to_all(blocks, 'ctx', split_axis=0, concat_axis=1, tiled=True)  16.5 us
    all_to_all x1, waiting for transfers between devices, a2a_reduce(): pieces = lax.all_to_all(values.reshape(count, -1), axes, 0, 0, tiled=True)  15 us
  transfers between devices with their start and end apart: 4, of which 4 were waited for; matrix products, arithmetic and copies ran while one was open for 1% of the time, Pallas kernels for 0%

profile of v1, /device:TPU:1, one launch (start us, length us, event | category | flops | bytes accessed | tf_op | source)
XLA Modules:
  0.0 447.6 jit_solution(10722027402071461247)
XLA Ops:
  6.2 10.1 %all-to-all-start = ((f32[128,2,256]{2,1,0:T(2,128)}), f32[128,2,256]{2,1,0:T(2,128)S(1)}, u32[]{:S(2)}, u32[]{:S(2)}) async-start(f32[128,2,256]{2,1,0:T(2,128)} %copy.40), calls=%async_computation | async-start | bytes 524288 | tf_op jit(solution)/shard_map/all_to_all | solution.py:29
  16.5 8.7 %all-to-all-done = f32[128,2,256]{2,1,0:T(2,128)S(1)} async-done(((f32[128,2,256]{2,1,0:T(2,128)}), f32[128,2,256]{2,1,0:T(2,128)S(1)}, u32[]{:S(2)}, u32[]{:S(2)}) %all-to-all-start) | async-done | bytes 262176 | tf_op jit(solution)/shard_map/all_to_all | solution.py:29
  27.5 29.2 %all_to_all.96 = f32[32,8,4,256]{3,2,1,0:T(4,128)S(1)} all-to-all(f32[32,8,4,256]{3,2,1,0:T(4,128)S(1)} %copy.43), channel_id=1, replica_groups=mesh['ctx'=16,'exp'=8,'rep'=2] {'ctx'}, dimensions={0} | all-to-all | bytes 2097152 | tf_op jit(solution)/shard_map/all_to_all | solution.py:29
  62.6 6.4 %all-to-all-start.2 = ((f32[128,2,2,256]{3,2,1,0:T(2,128)}), f32[128,2,2,256]{3,2,1,0:T(2,128)}, u32[]{:S(2)}, u32[]{:S(2)}) async-start(f32[128,2,2,256]{3,2,1,0:T(2,128)} %copy.45), calls=%async_computation.2 | async-start | bytes 1048576 | tf_op jit(solution)/shard_map/all_to_all | solution.py:29
  69.2 12.9 %all-to-all-done.2 = f32[128,2,2,256]{3,2,1,0:T(2,128)} async-done(((f32[128,2,2,256]{3,2,1,0:T(2,128)}), f32[128,2,2,256]{3,2,1,0:T(2,128)}, u32[]{:S(2)}, u32[]{:S(2)}) %all-to-all-start.2) | async-done | bytes 524320 | tf_op jit(solution)/shard_map/all_to_all | solution.py:29
  82.1 2.1 copy.46
  84.2 2.2 all_to_all.76
  89.3 13.4 %all_to_all.97 = f32[16,8,256]{2,1,0:T(8,128)S(1)} all-to-all(f32[16,8,256]{2,1,0:T(8,128)S(1)} %copy.47), channel_id=1, replica_groups=mesh['ctx'=16,'exp'=8,'rep'=2] {'ctx'}, dimensions={0} | all-to-all | bytes 262144 | tf_op jit(solution)/shard_map/all_to_all | solution.py:29
  102.8 2.6 fusion.72
  105.4 3.5 all_to_all.85
  108.8 7.6 %all-to-all-start.4 = ((f32[8,1,32768]{2,1,0:T(1,128)}), f32[8,1,32768]{2,1,0:T(1,128)}, u32[]{:S(2)}, u32[]{:S(2)}) async-start(f32[8,1,32768]{2,1,0:T(1,128)} %all_to_all.85), calls=%async_computation.4 | async-start | bytes 2097152 | tf_op jit(solution)/shard_map/all_to_all | solution.py:34
  116.5 15.0 %all-to-all-done.4 = f32[8,1,32768]{2,1,0:T(1,128)} async-done(((f32[8,1,32768]{2,1,0:T(1,128)}), f32[8,1,32768]{2,1,0:T(1,128)}, u32[]{:S(2)}, u32[]{:S(2)}) %all-to-all-start.4) | async-done | bytes 1048608 | tf_op jit(solution)/shard_map/all_to_all | solution.py:34
  135.4 103.9 %all_to_all.98 = bf16[128,8,2048]{2,1,0:T(8,128)(2,1)S(1)} all-to-all(bf16[128,8,2048]{2,1,0:T(8,128)(2,1)S(1)} %bitcast.172), channel_id=1, replica_groups=mesh['ctx'=16,'exp'=8,'rep'=2] {'ctx','exp'}, dimensions={0} | all-to-all | bytes 8388608 | tf_op jit(solution)/shard_map/all_to_all | solution.py:48
  241.2 2.3 fusion.2
  243.5 9.4 %convert_bitcast_fusion = bf16[128,8,2048]{2,1,0:T(8,128)(2,1)} fusion(bf16[1,256,2048]{2,1,0:T(8,128)(2,1)} %param.29, bf16[128,8,2048]{2,1,0:T(8,128)(2,1)} %copy-done.1, bf16[1,2048,256]{2,1,0:T(8,128)(2,1)} %param.28, f32[1024,256]{1,0:T(8,128)} %fusion.2), kind=kOutput, calls=%fused_computation.7 | convolution fusion | flops 2151153664 | bytes 11534336 | tf_op jit(solution)/shard_map/dot_general | solution.py:164
  252.9 6.9 %all-to-all-start.6 = ((bf16[128,8,2048]{2,1,0:T(8,128)(2,1)}), bf16[128,8,2048]{2,1,0:T(8,128)(2,1)}, u32[]{:S(2)}, u32[]{:S(2)}) async-start(bf16[128,8,2048]{2,1,0:T(8,128)(2,1)} %convert_bitcast_fusion), calls=%async_computation.6 | async-start | bytes 8388608 | tf_op jit(solution)/shard_map/all_to_all | solution.py:48
  262.8 94.0 %all-to-all-done.6 = bf16[128,8,2048]{2,1,0:T(8,128)(2,1)} async-done(((bf16[128,8,2048]{2,1,0:T(8,128)(2,1)}), bf16[128,8,2048]{2,1,0:T(8,128)(2,1)}, u32[]{:S(2)}, u32[]{:S(2)}) %all-to-all-start.6) | async-done | bytes 4194336 | tf_op jit(solution)/shard_map/all_to_all | solution.py:48
  356.8 3.0 reduce_sum.61
  362.7 2.7 fusion.18
  365.5 3.2 all_to_all.86
  368.7 35.5 %all_to_all.99 = f32[256,1,896]{2,1,0:T(1,128)} all-to-all(f32[256,1,896]{2,1,0:T(1,128)} %all_to_all.86), channel_id=1, replica_groups=mesh['ctx'=16,'exp'=8,'rep'=2] {'ctx','exp','rep'}, dimensions={0} | all-to-all | bytes 1835008 | tf_op jit(solution)/shard_map/all_to_all | solution.py:34
  406.4 34.6 %all_to_all.100 = f32[256,1,896]{2,1,0:T(1,128)} all-to-all(f32[256,1,896]{2,1,0:T(1,128)S(1)} %broadcast_in_dim.22), channel_id=1, replica_groups=mesh['ctx'=16,'exp'=8,'rep'=2] {'ctx','exp','rep'}, dimensions={0} | all-to-all | bytes 1835008 | tf_op jit(solution)/shard_map/all_to_all | solution.py:44
  441.0 4.3 reduce.3
  445.3 2.3 reshape.241
  (80 shorter events, 30.7 us)
Async XLA Ops:
  0.6 2.1 copy-start
  0.6 4.5 %copy-start.10 = (f32[256]{0:T(256)S(1)}, f32[256]{0:T(256)}, u32[]{:S(2)}) copy-start(f32[256]{0:T(256)} %param.22) | copy-start | bytes 3076
  0.7 4.5 %copy-start.4 = (f32[128,256]{1,0:T(8,128)S(1)}, f32[128,256]{1,0:T(8,128)}, u32[]{:S(2)}) copy-start(f32[128,256]{1,0:T(8,128)} %param.21) | copy-start | bytes 393220
  4.4 0.8 copy-start.2
  6.2 18.9 %all-to-all-start = ((f32[128,2,256]{2,1,0:T(2,128)}), f32[128,2,256]{2,1,0:T(2,128)S(1)}, u32[]{:S(2)}, u32[]{:S(2)}) async-start(f32[128,2,256]{2,1,0:T(2,128)} %copy.40), calls=%async_computation | async-start | bytes 524288 | tf_op jit(solution)/shard_map/all_to_all | solution.py:29
  61.3 41.5 %copy-start.8 = (f32[256]{0:T(256)S(1)}, f32[256]{0:T(256)}, u32[]{:S(2)}) copy-start(f32[256]{0:T(256)} %param.23) | copy-start | bytes 3076
  62.6 19.5 %all-to-all-start.2 = ((f32[128,2,2,256]{3,2,1,0:T(2,128)}), f32[128,2,2,256]{3,2,1,0:T(2,128)}, u32[]{:S(2)}, u32[]{:S(2)}) async-start(f32[128,2,2,256]{3,2,1,0:T(2,128)} %copy.45), calls=%async_computation.2 | async-start | bytes 1048576 | tf_op jit(solution)/shard_map/all_to_all | solution.py:29
  86.4 30.0 %copy-start.5 = (s32[1,16,2]{1,2,0:T(2,128)S(1)}, s32[1,16,2]{1,2,0:T(2,128)}, u32[]{:S(2)}) copy-start(s32[1,16,2]{1,2,0:T(2,128)} %param.30) | copy-start | bytes 388
  86.4 30.0 %copy-start.9 = (s32[1,16,2]{1,2,0:T(2,128)S(1)}, s32[1,16,2]{1,2,0:T(2,128)}, u32[]{:S(2)}) copy-start(s32[1,16,2]{1,2,0:T(2,128)} %param.31) | copy-start | bytes 388
  102.8 31.8 %copy-start.7 = (f32[2048]{0:T(1024)S(1)}, f32[2048]{0:T(1024)}, u32[]{:S(2)}) copy-start(f32[2048]{0:T(1024)} %param.25) | copy-start | bytes 24580
  108.8 22.7 %all-to-all-start.4 = ((f32[8,1,32768]{2,1,0:T(1,128)}), f32[8,1,32768]{2,1,0:T(1,128)}, u32[]{:S(2)}, u32[]{:S(2)}) async-start(f32[8,1,32768]{2,1,0:T(1,128)} %all_to_all.85), calls=%async_computation.4 | async-start | bytes 2097152 | tf_op jit(solution)/shard_map/all_to_all | solution.py:34
  135.4 105.8 %copy-start.11 = (bf16[1,2048,256]{2,1,0:T(8,128)(2,1)S(1)}, bf16[1,2048,256]{2,1,0:T(8,128)(2,1)}, u32[]{:S(2)}) copy-start(bf16[1,2048,256]{2,1,0:T(8,128)(2,1)} %param.27) | copy-start | bytes 3145732
  239.2 2.0 copy-start.1
  252.9 8.2 %copy-start.12 = (bf16[2048,8]{0,1:T(8,128)(2,1)S(1)}, bf16[2048,8]{0,1:T(8,128)(2,1)}, u32[]{:S(2)}) copy-start(bf16[2048,8]{0,1:T(8,128)(2,1)} %param.26) | copy-start | bytes 98308
  252.9 103.9 %all-to-all-start.6 = ((bf16[128,8,2048]{2,1,0:T(8,128)(2,1)}), bf16[128,8,2048]{2,1,0:T(8,128)(2,1)}, u32[]{:S(2)}, u32[]{:S(2)}) async-start(bf16[128,8,2048]{2,1,0:T(8,128)(2,1)} %convert_bitcast_fusion), calls=%async_computation.6 | async-start | bytes 8388608 | tf_op jit(solution)/shard_map/all_to_all | solution.py:48
  262.0 100.7 %copy-start.6 = (f32[1,16,112]{2,1,0:T(8,128)S(1)}, f32[1,16,112]{2,1,0:T(8,128)}, u32[]{:S(2)}) copy-start(f32[1,16,112]{2,1,0:T(8,128)} %param.33) | copy-start | bytes 21508
  362.7 78.2 %copy-start.3 = (bf16[16,2048]{1,0:T(8,128)(2,1)}, bf16[16,2048]{1,0:T(8,128)(2,1)S(1)}, u32[]{:S(2)}) copy-start(bf16[16,2048]{1,0:T(8,128)(2,1)S(1)} %fusion.60) | copy-start | bytes 196612

commit v2 on v1

--- a/solution.py
+++ b/solution.py
@@ -29,19 +29,25 @@
     return lax.all_to_all(blocks, "ctx", split_axis=0, concat_axis=1, tiled=True)
 
 
-def a2a_reduce(values, axes):
+def a2a_reduce(values, axes, wire=None):
     count = lax.axis_size(axes)
-    pieces = lax.all_to_all(values.reshape(count, -1), axes, 0, 0, tiled=True)
-    return jnp.sum(pieces, axis=0)
-
-
-def a2a_allreduce(values, axes):
+    sent = values.reshape(count, -1)
+    if wire is not None:
+        sent = sent.astype(wire)
+    pieces = lax.all_to_all(sent, axes, 0, 0, tiled=True)
+    return jnp.sum(pieces.astype(jnp.float32), axis=0)
+
+
+def a2a_allreduce(values, axes, wire=None):
     count = lax.axis_size(axes)
     if values.size % count:
         return lax.psum(values, axes)
-    mine = a2a_reduce(values, axes)
+    mine = a2a_reduce(values, axes, wire)
+    if wire is not None:
+        mine = mine.astype(wire)
     spread = jnp.broadcast_to(mine[None], (count,) + mine.shape)
-    return lax.all_to_all(spread, axes, 0, 0, tiled=True).reshape(values.shape)
+    gathered = lax.all_to_all(spread, axes, 0, 0, tiled=True)
+    return gathered.astype(jnp.float32).reshape(values.shape)
 
 
 def token_move(blocks):
@@ -184,7 +190,7 @@
     local_grad = jnp.einsum(
         "to,td->od", usage_grad, block_final, preferred_element_type=jnp.float32
     )
-    head_total = a2a_allreduce(local_grad, ("ctx", "exp", "rep"))
+    head_total = a2a_allreduce(local_grad, ("ctx", "exp", "rep"), jnp.bfloat16)
     return (block_final[None], head_total)
 
 

time: 449 us -> 467 us (1.040); the launches traced: 448 us -> 458 us
  blocking collectives: 217 us -> 203 us
  local copies, waits for them, and re-layouts: 24.2 us -> 36.7 us
  other arithmetic: 16.4 us -> 27.3 us
    all_to_all x2, blocking collectives: 70.1 us -> 55.9 us  [the longest x1 28.1 us: a2a_allreduce(): gathered = lax.all_to_all(spread, axes, 0, 0, tiled=True)]
    unnamed x26 -> x30, local copies, waits for them, and re-layouts: 3.41 us -> 15.3 us
    convert_element_type x0 -> x2, other arithmetic: none -> 9.88 us  [the longest x1 5.15 us: a2a_reduce(): sent = sent.astype(wire)]
    convert_element_type x0 -> x3, local copies, waits for them, and re-layouts: none -> 5.34 us  [the longest x2 3 us: a2a_reduce(): sent = sent.astype(wire)]
    broadcast_in_dim x0 -> x1, other arithmetic: none -> 5.15 us  [a2a_allreduce(): spread = jnp.broadcast_to(mine[None], (count,) + mine.shape)]
where the time goes in v2:
time: 467 us; the launch traced here: 458 us
  blocking collectives  203 us (43%)
  waiting for transfers between devices  131 us (28%)
  local copies, waits for them, and re-layouts  36.7 us (8%)
  starting transfers between devices  31 us (7%)
  matrix products  27.6 us (6%)
  other arithmetic  27.3 us (6%)
    all_to_all x1, blocking collectives, token_move(): lax.all_to_all(blocks, ('ctx', 'exp'), split_axis=0, concat_axis=0, tiled...  104 us
    all_to_all x1, waiting for transfers between devices, token_move(): lax.all_to_all(blocks, ('ctx', 'exp'), split_axis=0, concat_axis=0, tiled...  94.2 us
    all_to_all x2, blocking collectives, spectra_move(): lax.all_to_all(blocks, 'ctx', split_axis=0, concat_axis=1, tiled=True)  42.8 us
    all_to_all x1, blocking collectives, a2a_allreduce(): gathered = lax.all_to_all(spread, axes, 0, 0, tiled=True)  28.1 us
    all_to_all x1, blocking collectives, a2a_reduce(): pieces = lax.all_to_all(sent, axes, 0, 0, tiled=True)  27.8 us
    all_to_all x2, waiting for transfers between devices, spectra_move(): lax.all_to_all(blocks, 'ctx', split_axis=0, concat_axis=1, tiled=True)  21.6 us
    all_to_all x2, starting transfers between devices, spectra_move(): lax.all_to_all(blocks, 'ctx', split_axis=0, concat_axis=1, tiled=True)  16.6 us
    unnamed x30, local copies, waits for them, and re-layouts  15.3 us
  transfers between devices with their start and end apart: 4, of which 4 were waited for; matrix products, arithmetic and copies ran while one was open for 1% of the time, Pallas kernels for 0%

profile of v2, /device:TPU:1, one launch (start us, length us, event | category | flops | bytes accessed | tf_op | source)
XLA Modules:
  0.0 457.6 jit_solution(1425233561857475558)
XLA Ops:
  6.2 10.1 %all-to-all-start = ((f32[128,2,256]{2,1,0:T(2,128)}), f32[128,2,256]{2,1,0:T(2,128)S(1)}, u32[]{:S(2)}, u32[]{:S(2)}) async-start(f32[128,2,256]{2,1,0:T(2,128)} %copy.40), calls=%async_computation | async-start | bytes 524288 | tf_op jit(solution)/shard_map/all_to_all | solution.py:29
  16.5 8.7 %all-to-all-done = f32[128,2,256]{2,1,0:T(2,128)S(1)} async-done(((f32[128,2,256]{2,1,0:T(2,128)}), f32[128,2,256]{2,1,0:T(2,128)S(1)}, u32[]{:S(2)}, u32[]{:S(2)}) %all-to-all-start) | async-done | bytes 262176 | tf_op jit(solution)/shard_map/all_to_all | solution.py:29
  27.5 29.2 %all_to_all.92 = f32[32,8,4,256]{3,2,1,0:T(4,128)S(1)} all-to-all(f32[32,8,4,256]{3,2,1,0:T(4,128)S(1)} %copy.43), channel_id=1, replica_groups=mesh['ctx'=16,'exp'=8,'rep'=2] {'ctx'}, dimensions={0} | all-to-all | bytes 2097152 | tf_op jit(solution)/shard_map/all_to_all | solution.py:29
  62.6 6.4 %all-to-all-start.2 = ((f32[128,2,2,256]{3,2,1,0:T(2,128)}), f32[128,2,2,256]{3,2,1,0:T(2,128)}, u32[]{:S(2)}, u32[]{:S(2)}) async-start(f32[128,2,2,256]{3,2,1,0:T(2,128)} %copy.45), calls=%async_computation.2 | async-start | bytes 1048576 | tf_op jit(solution)/shard_map/all_to_all | solution.py:29
  69.2 12.9 %all-to-all-done.2 = f32[128,2,2,256]{3,2,1,0:T(2,128)} async-done(((f32[128,2,2,256]{3,2,1,0:T(2,128)}), f32[128,2,2,256]{3,2,1,0:T(2,128)}, u32[]{:S(2)}, u32[]{:S(2)}) %all-to-all-start.2) | async-done | bytes 524320 | tf_op jit(solution)/shard_map/all_to_all | solution.py:29
  89.3 13.6 %all_to_all.93 = f32[16,8,256]{2,1,0:T(8,128)S(1)} all-to-all(f32[16,8,256]{2,1,0:T(8,128)S(1)} %copy.47), channel_id=1, replica_groups=mesh['ctx'=16,'exp'=8,'rep'=2] {'ctx'}, dimensions={0} | all-to-all | bytes 262144 | tf_op jit(solution)/shard_map/all_to_all | solution.py:29
  102.9 2.6 fusion.71
  105.5 3.5 all_to_all.82
  109.0 7.6 %all-to-all-start.4 = ((f32[8,1,32768]{2,1,0:T(1,128)}), f32[8,1,32768]{2,1,0:T(1,128)}, u32[]{:S(2)}, u32[]{:S(2)}) async-start(f32[8,1,32768]{2,1,0:T(1,128)} %all_to_all.82), calls=%async_computation.4 | async-start | bytes 2097152 | tf_op jit(solution)/shard_map/all_to_all | solution.py:37
  116.7 15.0 %all-to-all-done.4 = f32[8,1,32768]{2,1,0:T(1,128)} async-done(((f32[8,1,32768]{2,1,0:T(1,128)}), f32[8,1,32768]{2,1,0:T(1,128)}, u32[]{:S(2)}, u32[]{:S(2)}) %all-to-all-start.4) | async-done | bytes 1048608 | tf_op jit(solution)/shard_map/all_to_all | solution.py:37
  135.5 103.9 %all_to_all.94 = bf16[128,8,2048]{2,1,0:T(8,128)(2,1)S(1)} all-to-all(bf16[128,8,2048]{2,1,0:T(8,128)(2,1)S(1)} %bitcast.172), channel_id=1, replica_groups=mesh['ctx'=16,'exp'=8,'rep'=2] {'ctx','exp'}, dimensions={0} | all-to-all | bytes 8388608 | tf_op jit(solution)/shard_map/all_to_all | solution.py:54
  243.7 9.4 %convert_bitcast_fusion = bf16[128,8,2048]{2,1,0:T(8,128)(2,1)} fusion(bf16[1,256,2048]{2,1,0:T(8,128)(2,1)} %param.29, bf16[128,8,2048]{2,1,0:T(8,128)(2,1)} %copy-done.1, bf16[1,2048,256]{2,1,0:T(8,128)(2,1)} %param.28, f32[1024,256]{1,0:T(8,128)} %fusion.2), kind=kOutput, calls=%fused_computation.7 | convolution fusion | flops 2151153664 | bytes 11534336 | tf_op jit(solution)/shard_map/dot_general | solution.py:170
  253.0 6.9 %all-to-all-start.6 = ((bf16[128,8,2048]{2,1,0:T(8,128)(2,1)}), bf16[128,8,2048]{2,1,0:T(8,128)(2,1)}, u32[]{:S(2)}, u32[]{:S(2)}) async-start(bf16[128,8,2048]{2,1,0:T(8,128)(2,1)} %convert_bitcast_fusion), calls=%async_computation.6 | async-start | bytes 8388608 | tf_op jit(solution)/shard_map/all_to_all | solution.py:54
  262.9 94.2 %all-to-all-done.6 = bf16[128,8,2048]{2,1,0:T(8,128)(2,1)} async-done(((bf16[128,8,2048]{2,1,0:T(8,128)(2,1)}), bf16[128,8,2048]{2,1,0:T(8,128)(2,1)}, u32[]{:S(2)}, u32[]{:S(2)}) %all-to-all-start.6) | async-done | bytes 4194336 | tf_op jit(solution)/shard_map/all_to_all | solution.py:54
  357.2 3.0 reduce_sum.64
  363.1 2.6 convolution_convert_fusion
  365.7 2.4 convert_element_type.147
  368.7 5.1 %reduce.6 = bf16[256,896]{1,0:T(8,128)(2,1)} reduce(bf16[256,1,896]{2,1,0:T(2,128)(2,1)} %convert_element_type.147, bf16[]{:T(256)} %broadcast.359), dimensions={1}, to_apply=%convert_element_type.147.reduce_sub_computation | reduce | bytes 917506 | tf_op jit(solution)/shard_map/convert_element_type | solution.py:36
  376.1 27.8 %all_to_all.95 = bf16[256,2,448]{2,1,0:T(2,128)(2,1)} all-to-all(bf16[256,2,448]{2,1,0:T(2,128)(2,1)} %reshape.290), channel_id=1, replica_groups=mesh['ctx'=16,'exp'=8,'rep'=2] {'ctx','exp','rep'}, dimensions={0} | all-to-all | bytes 917504 | tf_op jit(solution)/shard_map/all_to_all | solution.py:37
  403.8 3.7 reshape.291
  410.9 5.1 %reduce.7 = bf16[256,896]{1,0:T(8,128)(2,1)} reduce(bf16[256,1,896]{2,1,0:T(2,128)(2,1)} %broadcast_in_dim.22, bf16[]{:T(256)} %broadcast.359), dimensions={1}, to_apply=%broadcast_in_dim.22.reduce_sub_computation | reduce | bytes 917506 | tf_op jit(solution)/shard_map/broadcast_in_dim | solution.py:48
  418.3 28.1 %all_to_all.96 = bf16[256,2,448]{2,1,0:T(2,128)(2,1)} all-to-all(bf16[256,2,448]{2,1,0:T(2,128)(2,1)} %reshape.292), channel_id=1, replica_groups=mesh['ctx'=16,'exp'=8,'rep'=2] {'ctx','exp','rep'}, dimensions={0} | all-to-all | bytes 917504 | tf_op jit(solution)/shard_map/all_to_all | solution.py:49
  446.4 3.7 reshape.293
  450.1 4.7 %convert_reduce_fusion = f32[256,896]{1,0:T(8,128)} fusion(bf16[256,1,896]{2,1,0:T(2,128)(2,1)} %reshape.293), kind=kLoop, calls=%fused_computation.42 | loop fusion | flops 229376 | bytes 1376256 | tf_op jit(solution)/shard_map/convert_element_type | solution.py:50
  (87 shorter events, 45.9 us)
Async XLA Ops:
  0.6 2.1 copy-start
  0.6 4.5 copy-start.10
  0.7 4.5 copy-start.4
  4.4 0.8 copy-start.2
  6.2 18.9 %all-to-all-start = ((f32[128,2,256]{2,1,0:T(2,128)}), f32[128,2,256]{2,1,0:T(2,128)S(1)}, u32[]{:S(2)}, u32[]{:S(2)}) async-start(f32[128,2,256]{2,1,0:T(2,128)} %copy.40), calls=%async_computation | async-start | bytes 524288 | tf_op jit(solution)/shard_map/all_to_all | solution.py:29
  61.3 41.6 %copy-start.8 = (f32[256]{0:T(256)S(1)}, f32[256]{0:T(256)}, u32[]{:S(2)}) copy-start(f32[256]{0:T(256)} %param.23) | copy-start | bytes 3076
  62.6 19.5 %all-to-all-start.2 = ((f32[128,2,2,256]{3,2,1,0:T(2,128)}), f32[128,2,2,256]{3,2,1,0:T(2,128)}, u32[]{:S(2)}, u32[]{:S(2)}) async-start(f32[128,2,2,256]{3,2,1,0:T(2,128)} %copy.45), calls=%async_computation.2 | async-start | bytes 1048576 | tf_op jit(solution)/shard_map/all_to_all | solution.py:29
  86.4 30.2 %copy-start.5 = (s32[1,16,2]{1,2,0:T(2,128)S(1)}, s32[1,16,2]{1,2,0:T(2,128)}, u32[]{:S(2)}) copy-start(s32[1,16,2]{1,2,0:T(2,128)} %param.30) | copy-start | bytes 388
  86.4 30.2 %copy-start.9 = (s32[1,16,2]{1,2,0:T(2,128)S(1)}, s32[1,16,2]{1,2,0:T(2,128)}, u32[]{:S(2)}) copy-start(s32[1,16,2]{1,2,0:T(2,128)} %param.31) | copy-start | bytes 388
  102.9 31.8 %copy-start.7 = (f32[2048]{0:T(1024)S(1)}, f32[2048]{0:T(1024)}, u32[]{:S(2)}) copy-start(f32[2048]{0:T(1024)} %param.25) | copy-start | bytes 24580
  109.0 22.7 %all-to-all-start.4 = ((f32[8,1,32768]{2,1,0:T(1,128)}), f32[8,1,32768]{2,1,0:T(1,128)}, u32[]{:S(2)}, u32[]{:S(2)}) async-start(f32[8,1,32768]{2,1,0:T(1,128)} %all_to_all.82), calls=%async_computation.4 | async-start | bytes 2097152 | tf_op jit(solution)/shard_map/all_to_all | solution.py:37
  135.5 105.9 %copy-start.11 = (bf16[1,2048,256]{2,1,0:T(8,128)(2,1)S(1)}, bf16[1,2048,256]{2,1,0:T(8,128)(2,1)}, u32[]{:S(2)}) copy-start(bf16[1,2048,256]{2,1,0:T(8,128)(2,1)} %param.27) | copy-start | bytes 3145732
  239.4 2.0 copy-start.1
  253.0 8.2 %copy-start.12 = (bf16[2048,8]{0,1:T(8,128)(2,1)S(1)}, bf16[2048,8]{0,1:T(8,128)(2,1)}, u32[]{:S(2)}) copy-start(bf16[2048,8]{0,1:T(8,128)(2,1)} %param.26) | copy-start | bytes 98308
  253.0 104.1 %all-to-all-start.6 = ((bf16[128,8,2048]{2,1,0:T(8,128)(2,1)}), bf16[128,8,2048]{2,1,0:T(8,128)(2,1)}, u32[]{:S(2)}, u32[]{:S(2)}) async-start(bf16[128,8,2048]{2,1,0:T(8,128)(2,1)} %convert_bitcast_fusion), calls=%async_computation.6 | async-start | bytes 8388608 | tf_op jit(solution)/shard_map/all_to_all | solution.py:54
  262.2 100.9 %copy-start.6 = (f32[1,16,112]{2,1,0:T(8,128)S(1)}, f32[1,16,112]{2,1,0:T(8,128)}, u32[]{:S(2)}) copy-start(f32[1,16,112]{2,1,0:T(8,128)} %param.33) | copy-start | bytes 21508
  363.1 47.8 %copy-start.3 = (bf16[16,2048]{1,0:T(8,128)(2,1)}, bf16[16,2048]{1,0:T(8,128)(2,1)S(1)}, u32[]{:S(2)}) copy-start(bf16[16,2048]{1,0:T(8,128)(2,1)S(1)} %fusion.59) | copy-start | bytes 196612

commit v3 on v2

--- a/solution.py
+++ b/solution.py
@@ -31,7 +31,7 @@
 
 def a2a_reduce(values, axes, wire=None):
     count = lax.axis_size(axes)
-    sent = values.reshape(count, -1)
+    sent = values.reshape((count, -1) + values.shape[1:])
     if wire is not None:
         sent = sent.astype(wire)
     pieces = lax.all_to_all(sent, axes, 0, 0, tiled=True)
@@ -40,7 +40,7 @@
 
 def a2a_allreduce(values, axes, wire=None):
     count = lax.axis_size(axes)
-    if values.size % count:
+    if values.shape[0] % count:
         return lax.psum(values, axes)
     mine = a2a_reduce(values, axes, wire)
     if wire is not None:
@@ -137,9 +137,7 @@
     convolved = causal_convolve(source, shaped)
     gated_rows = (projected[:, 2] * (convolved + conv_bias[None, :] * source)).astype(jnp.bfloat16)
     mixed_full = jnp.dot(gated_rows, w_out, preferred_element_type=jnp.float32)
-    mixed_sum = a2a_reduce(mixed_full.reshape(exp_count, own_rows * model_width), "exp").reshape(
-        own_rows, model_width
-    )
+    mixed_sum = a2a_reduce(mixed_full, "exp")
     residual_rows = lax.dynamic_slice_in_dim(local_x, exp_pos * own_rows, own_rows, 0)
     hidden_state = stored(residual_rows.astype(jnp.float32) + mixed_sum)
     routed_in = rms_scale(hidden_state, norm2_gain)
@@ -188,9 +186,9 @@
     loss_scale = 1.0 / math.sqrt(all_tokens)
     usage_grad = ((usage_prob - targets[0]) * loss_scale).astype(jnp.bfloat16)
     local_grad = jnp.einsum(
-        "to,td->od", usage_grad, block_final, preferred_element_type=jnp.float32
-    )
-    head_total = a2a_allreduce(local_grad, ("ctx", "exp", "rep"), jnp.bfloat16)
+        "td,to->do", block_final, usage_grad, preferred_element_type=jnp.float32
+    )
+    head_total = a2a_allreduce(local_grad, ("ctx", "exp", "rep"), jnp.bfloat16).T
     return (block_final[None], head_total)
 
 

time: 467 us -> 425 us (0.910); the launches traced: 458 us -> 423 us
  local copies, waits for them, and re-layouts: 36.7 us -> 18.4 us
  other arithmetic: 27.3 us -> 13.3 us
    unnamed x30 -> x25, local copies, waits for them, and re-layouts: 15.3 us -> 5.13 us
    convert_element_type x2 -> x1, other arithmetic: 9.88 us -> 0.71 us  [shards(): (projected[:, 2] * (convolved + conv_bias[None, :] * source)).astype(jnp....]
    broadcast_in_dim x1 -> x0, other arithmetic: 5.15 us -> none  [a2a_allreduce(): spread = jnp.broadcast_to(mine[None], (count,) + mine.shape)]
where the time goes in v3:
time: 425 us; the launch traced here: 423 us
  blocking collectives  201 us (47%)
  waiting for transfers between devices  131 us (31%)
  starting transfers between devices  30.8 us (7%)
  matrix products  28.3 us (7%)
  local copies, waits for them, and re-layouts  18.4 us (4%)
  other arithmetic  13.3 us (3%)
    all_to_all x1, blocking collectives, token_move(): lax.all_to_all(blocks, ('ctx', 'exp'), split_axis=0, concat_axis=0, tiled...  104 us
    all_to_all x1, waiting for transfers between devices, token_move(): lax.all_to_all(blocks, ('ctx', 'exp'), split_axis=0, concat_axis=0, tiled...  94.3 us
    all_to_all x2, blocking collectives, spectra_move(): lax.all_to_all(blocks, 'ctx', split_axis=0, concat_axis=1, tiled=True)  42.7 us
    all_to_all x1, blocking collectives, a2a_reduce(): pieces = lax.all_to_all(sent, axes, 0, 0, tiled=True)  27.8 us
    all_to_all x1, blocking collectives, a2a_allreduce(): gathered = lax.all_to_all(spread, axes, 0, 0, tiled=True)  26.3 us
    all_to_all x2, waiting for transfers between devices, spectra_move(): lax.all_to_all(blocks, 'ctx', split_axis=0, concat_axis=1, tiled=True)  21.6 us
    all_to_all x2, starting transfers between devices, spectra_move(): lax.all_to_all(blocks, 'ctx', split_axis=0, concat_axis=1, tiled=True)  16.5 us
    all_to_all x1, waiting for transfers between devices, a2a_reduce(): pieces = lax.all_to_all(sent, axes, 0, 0, tiled=True)  15 us
  transfers between devices with their start and end apart: 4, of which 4 were waited for; matrix products, arithmetic and copies ran while one was open for 1% of the time, Pallas kernels for 0%

profile of v3, /device:TPU:1, one launch (start us, length us, event | category | flops | bytes accessed | tf_op | source)
XLA Modules:
  0.0 423.5 jit_solution(10328723275536875362)
XLA Ops:
  2.7 1.7 fusion.38
  6.1 10.1 %all-to-all-start = ((f32[128,2,256]{2,1,0:T(2,128)}), f32[128,2,256]{2,1,0:T(2,128)S(1)}, u32[]{:S(2)}, u32[]{:S(2)}) async-start(f32[128,2,256]{2,1,0:T(2,128)} %copy.41), calls=%async_computation | async-start | bytes 524288 | tf_op jit(solution)/shard_map/all_to_all | solution.py:29
  16.3 8.7 %all-to-all-done = f32[128,2,256]{2,1,0:T(2,128)S(1)} async-done(((f32[128,2,256]{2,1,0:T(2,128)}), f32[128,2,256]{2,1,0:T(2,128)S(1)}, u32[]{:S(2)}, u32[]{:S(2)}) %all-to-all-start) | async-done | bytes 262176 | tf_op jit(solution)/shard_map/all_to_all | solution.py:29
  27.4 29.2 %all_to_all.85 = f32[32,8,4,256]{3,2,1,0:T(4,128)S(1)} all-to-all(f32[32,8,4,256]{3,2,1,0:T(4,128)S(1)} %copy.44), channel_id=1, replica_groups=mesh['ctx'=16,'exp'=8,'rep'=2] {'ctx'}, dimensions={0} | all-to-all | bytes 2097152 | tf_op jit(solution)/shard_map/all_to_all | solution.py:29
  62.5 6.4 %all-to-all-start.2 = ((f32[128,2,2,256]{3,2,1,0:T(2,128)}), f32[128,2,2,256]{3,2,1,0:T(2,128)}, u32[]{:S(2)}, u32[]{:S(2)}) async-start(f32[128,2,2,256]{3,2,1,0:T(2,128)} %copy.46), calls=%async_computation.2 | async-start | bytes 1048576 | tf_op jit(solution)/shard_map/all_to_all | solution.py:29
  69.0 12.9 %all-to-all-done.2 = f32[128,2,2,256]{3,2,1,0:T(2,128)} async-done(((f32[128,2,2,256]{3,2,1,0:T(2,128)}), f32[128,2,2,256]{3,2,1,0:T(2,128)}, u32[]{:S(2)}, u32[]{:S(2)}) %all-to-all-start.2) | async-done | bytes 524320 | tf_op jit(solution)/shard_map/all_to_all | solution.py:29
  82.0 2.1 copy.47
  84.1 2.2 all_to_all.69
  89.2 13.4 %all_to_all.86 = f32[16,8,256]{2,1,0:T(8,128)S(1)} all-to-all(f32[16,8,256]{2,1,0:T(8,128)S(1)} %copy.48), channel_id=1, replica_groups=mesh['ctx'=16,'exp'=8,'rep'=2] {'ctx'}, dimensions={0} | all-to-all | bytes 262144 | tf_op jit(solution)/shard_map/all_to_all | solution.py:29
  103.3 2.5 fusion.27
  105.8 7.6 %all-to-all-start.4 = ((f32[8,16,2048]{2,1,0:T(8,128)}), f32[8,16,2048]{2,1,0:T(8,128)}, u32[]{:S(2)}, u32[]{:S(2)}) async-start(f32[8,16,2048]{2,1,0:T(8,128)} %fusion.27), calls=%async_computation.4 | async-start | bytes 2097152 | tf_op jit(solution)/shard_map/all_to_all | solution.py:37
  113.5 15.0 %all-to-all-done.4 = f32[8,16,2048]{2,1,0:T(8,128)} async-done(((f32[8,16,2048]{2,1,0:T(8,128)}), f32[8,16,2048]{2,1,0:T(8,128)}, u32[]{:S(2)}, u32[]{:S(2)}) %all-to-all-start.4) | async-done | bytes 1048608 | tf_op jit(solution)/shard_map/all_to_all | solution.py:37
  132.3 104.0 %all_to_all.87 = bf16[128,8,2048]{2,1,0:T(8,128)(2,1)S(1)} all-to-all(bf16[128,8,2048]{2,1,0:T(8,128)(2,1)S(1)} %bitcast.173), channel_id=1, replica_groups=mesh['ctx'=16,'exp'=8,'rep'=2] {'ctx','exp'}, dimensions={0} | all-to-all | bytes 8388608 | tf_op jit(solution)/shard_map/all_to_all | solution.py:54
  236.3 2.0 copy-done.1
  238.3 2.3 fusion.2
  240.6 9.4 %convert_bitcast_fusion = bf16[128,8,2048]{2,1,0:T(8,128)(2,1)} fusion(bf16[1,256,2048]{2,1,0:T(8,128)(2,1)} %param.29, bf16[128,8,2048]{2,1,0:T(8,128)(2,1)} %copy-done.1, bf16[1,2048,256]{2,1,0:T(8,128)(2,1)} %param.28, f32[1024,256]{1,0:T(8,128)} %fusion.2), kind=kOutput, calls=%fused_computation.7 | convolution fusion | flops 2151153664 | bytes 11534336 | tf_op jit(solution)/shard_map/dot_general | solution.py:168
  250.0 6.6 %all-to-all-start.6 = ((bf16[128,8,2048]{2,1,0:T(8,128)(2,1)}), bf16[128,8,2048]{2,1,0:T(8,128)(2,1)}, u32[]{:S(2)}, u32[]{:S(2)}) async-start(bf16[128,8,2048]{2,1,0:T(8,128)(2,1)} %convert_bitcast_fusion), calls=%async_computation.6 | async-start | bytes 8388608 | tf_op jit(solution)/shard_map/all_to_all | solution.py:54
  259.6 94.3 %all-to-all-done.6 = bf16[128,8,2048]{2,1,0:T(8,128)(2,1)} async-done(((bf16[128,8,2048]{2,1,0:T(8,128)(2,1)}), bf16[128,8,2048]{2,1,0:T(8,128)(2,1)}, u32[]{:S(2)}, u32[]{:S(2)}) %all-to-all-start.6) | async-done | bytes 4194336 | tf_op jit(solution)/shard_map/all_to_all | solution.py:54
  353.9 3.0 reduce_sum.64
  359.9 2.6 convolution_convert_fusion
  362.5 2.0 copy.51
  364.5 27.8 %all_to_all.88 = bf16[256,8,112]{2,1,0:T(8,128)(2,1)} all-to-all(bf16[256,8,112]{2,1,0:T(8,128)(2,1)} %bitcast.180), channel_id=1, replica_groups=mesh['ctx'=16,'exp'=8,'rep'=2] {'ctx','exp','rep'}, dimensions={0} | all-to-all | bytes 917504 | tf_op jit(solution)/shard_map/all_to_all | solution.py:37
  393.6 26.3 %all_to_all.89 = bf16[256,8,112]{2,1,0:T(8,128)(2,1)S(1)} all-to-all(bf16[256,8,112]{2,1,0:T(8,128)(2,1)S(1)} %broadcast_in_dim.22), channel_id=1, replica_groups=mesh['ctx'=16,'exp'=8,'rep'=2] {'ctx','exp','rep'}, dimensions={0} | all-to-all | bytes 917504 | tf_op jit(solution)/shard_map/all_to_all | solution.py:49
  421.0 2.5 copy.52
  (77 shorter events, 27.8 us)
Async XLA Ops:
  0.6 2.1 copy-start
  0.6 4.4 %copy-start.9 = (f32[256]{0:T(256)S(1)}, f32[256]{0:T(256)}, u32[]{:S(2)}) copy-start(f32[256]{0:T(256)} %param.22) | copy-start | bytes 3076
  0.7 4.4 %copy-start.4 = (f32[128,256]{1,0:T(8,128)S(1)}, f32[128,256]{1,0:T(8,128)}, u32[]{:S(2)}) copy-start(f32[128,256]{1,0:T(8,128)} %param.21) | copy-start | bytes 393220
  6.1 18.9 %all-to-all-start = ((f32[128,2,256]{2,1,0:T(2,128)}), f32[128,2,256]{2,1,0:T(2,128)S(1)}, u32[]{:S(2)}, u32[]{:S(2)}) async-start(f32[128,2,256]{2,1,0:T(2,128)} %copy.41), calls=%async_computation | async-start | bytes 524288 | tf_op jit(solution)/shard_map/all_to_all | solution.py:29
  61.1 41.5 %copy-start.3 = (f32[128,1,256]{2,0,1:T(8,128)S(1)}, f32[128,1,256]{2,0,1:T(8,128)}, u32[]{:S(2)}) copy-start(f32[128,1,256]{2,0,1:T(8,128)} %get-tuple-element.24) | copy-start | bytes 393220
  62.5 19.5 %all-to-all-start.2 = ((f32[128,2,2,256]{3,2,1,0:T(2,128)}), f32[128,2,2,256]{3,2,1,0:T(2,128)}, u32[]{:S(2)}, u32[]{:S(2)}) async-start(f32[128,2,2,256]{3,2,1,0:T(2,128)} %copy.46), calls=%async_computation.2 | async-start | bytes 1048576 | tf_op jit(solution)/shard_map/all_to_all | solution.py:29
  68.9 44.5 %copy-start.5 = (s32[1,16,2]{1,2,0:T(2,128)S(1)}, s32[1,16,2]{1,2,0:T(2,128)}, u32[]{:S(2)}) copy-start(s32[1,16,2]{1,2,0:T(2,128)} %param.30) | copy-start | bytes 388
  69.0 44.4 %copy-start.8 = (s32[1,16,2]{1,2,0:T(2,128)S(1)}, s32[1,16,2]{1,2,0:T(2,128)}, u32[]{:S(2)}) copy-start(s32[1,16,2]{1,2,0:T(2,128)} %param.31) | copy-start | bytes 388
  105.8 22.7 %all-to-all-start.4 = ((f32[8,16,2048]{2,1,0:T(8,128)}), f32[8,16,2048]{2,1,0:T(8,128)}, u32[]{:S(2)}, u32[]{:S(2)}) async-start(f32[8,16,2048]{2,1,0:T(8,128)} %fusion.27), calls=%async_computation.4 | async-start | bytes 2097152 | tf_op jit(solution)/shard_map/all_to_all | solution.py:37
  132.3 106.0 %copy-start.10 = (bf16[1,2048,256]{2,1,0:T(8,128)(2,1)S(1)}, bf16[1,2048,256]{2,1,0:T(8,128)(2,1)}, u32[]{:S(2)}) copy-start(bf16[1,2048,256]{2,1,0:T(8,128)(2,1)} %param.27) | copy-start | bytes 3145732
  236.3 2.0 copy-start.1
  250.0 8.0 %copy-start.7 = (f32[2048]{0:T(1024)S(1)}, f32[2048]{0:T(1024)}, u32[]{:S(2)}) copy-start(f32[2048]{0:T(1024)} %param.25) | copy-start | bytes 24580
  250.0 8.0 %copy-start.11 = (bf16[2048,8]{0,1:T(8,128)(2,1)S(1)}, bf16[2048,8]{0,1:T(8,128)(2,1)}, u32[]{:S(2)}) copy-start(bf16[2048,8]{0,1:T(8,128)(2,1)} %param.26) | copy-start | bytes 98308
  250.0 103.9 %all-to-all-start.6 = ((bf16[128,8,2048]{2,1,0:T(8,128)(2,1)}), bf16[128,8,2048]{2,1,0:T(8,128)(2,1)}, u32[]{:S(2)}, u32[]{:S(2)}) async-start(bf16[128,8,2048]{2,1,0:T(8,128)(2,1)} %convert_bitcast_fusion), calls=%async_computation.6 | async-start | bytes 8388608 | tf_op jit(solution)/shard_map/all_to_all | solution.py:54
  258.9 101.0 %copy-start.6 = (f32[1,16,112]{2,1,0:T(8,128)S(1)}, f32[1,16,112]{2,1,0:T(8,128)}, u32[]{:S(2)}) copy-start(f32[1,16,112]{2,1,0:T(8,128)} %param.33) | copy-start | bytes 21508
  359.8 63.6 %copy-start.2 = (bf16[16,2048]{1,0:T(8,128)(2,1)}, bf16[16,2048]{1,0:T(8,128)(2,1)S(1)}, u32[]{:S(2)}) copy-start(bf16[16,2048]{1,0:T(8,128)(2,1)S(1)} %fusion.61) | copy-start | bytes 196612
